TPU v7x, 512 devices: a whole 4x4x16 slice. The times are simulated.
512 devices in a mesh: dp: 64 (over z, y), fsdp: 8 (over x, core).
Axes of the slice: x: 4, y: 4, z: 16, core: 2. Of those that a mesh axis runs over, the one named last changes fastest.
Arguments:
- tokens: bfloat16 [65536, 2048], P('dp', 'fsdp'), may hold values from -6 to 6
- norm_gain: bfloat16 [2048], replicated, may hold values from 0.25 to 1.75
- query_gain: bfloat16 [128], replicated, as said below
- key_gain: bfloat16 [128], replicated, as said below
- w_query: bfloat16 [2048, 2048], P('dp', 'fsdp'), as said below
- w_key: bfloat16 [2048, 1024], P('dp', 'fsdp'), as said below
- w_value: bfloat16 [2048, 1024], P('dp', 'fsdp'), may hold values from -0.125 to 0.125
- w_out: bfloat16 [2048, 2048], P('dp', 'fsdp'), may hold values from -0.125 to 0.125
- prompt_lengths: int32 [64, 8], replicated, may hold values from 1 to 512, 1024 in all within a row
- span_group: int32 [64, 64], replicated, may hold values from 0 to 63, as said below
Outputs:
- attention_update: bfloat16 [65536, 2048], P('dp', 'fsdp')
- kv_cache: bfloat16 [65536, 8, 256], P('dp', 'fsdp')
Inputs may be any that keep to these rules, and one draw needn't show every extreme that they name: `prompt_lengths`: row g sums to 1024. `span_group`: row i names, in arrival order, the group of each of its 64 blocks of 16 rows; every group is named exactly 64 times in all; every row names exactly one group twice and leaves exactly one group out, and every group is the one named twice by exactly one row. `query_gain`: Positive. `key_gain`: Positive. `w_query`: entries of size about one over the square root of 2048. `w_key`: entries of size about one over the square root of 2048.
All inputs are finite; a program needn't handle non-finite values.
Results may differ from a plain program's by a relative error of at most 0.0075.
The roundings to bfloat16 on the way count: a program that leaves them out, or rounds other values in their place, can miss the bound.
Values may be sent and summed in bfloat16 or wider, within the bound.
No kernel may reach another device: no remote copies, remote signals or barrier semaphores. Data moves between devices by JAX's collectives and lax.ppermute only.
A program may use at most 64 MiB of HBM per device.

v0:
```python
import math
import jax
import jax.numpy as jnp
from jax import lax
from jax.sharding import PartitionSpec as P

QH = 16
KVH = 8
HD = 128
epsilon = 1e-06
rope_base = 1000000.0


def for_sending(x):

    def short(part):
        return part.astype(jnp.bfloat16) if part.dtype == jnp.float32 else part

    return jax.tree.map(short, x)


def head_norm(inputs, gains):
    inv_rms = lax.rsqrt(jnp.mean(inputs * inputs, axis=-1, keepdims=True) + epsilon)
    return inputs * inv_rms * gains.astype(jnp.float32)


def rotate(inputs, offsets):
    half_dim = inputs.shape[-1] // 2
    frequency = jnp.power(
        rope_base, -2.0 * jnp.arange(half_dim, dtype=jnp.float32) / inputs.shape[-1]
    )
    angles = offsets.astype(jnp.float32)[:, None] * frequency[None, :]
    cosine = jnp.cos(angles)[:, None, :]
    sine_part = jnp.sin(angles)[:, None, :]
    first_half = inputs[..., :half_dim]
    second = inputs[..., half_dim:]
    return jnp.concatenate(
        [first_half * cosine - second * sine_part, second * cosine + first_half * sine_part],
        axis=-1,
    )


def prompt_layout(lengths, group_rows):
    prompt_end = jnp.cumsum(lengths)
    begins = prompt_end - lengths
    position = jnp.arange(group_rows, dtype=jnp.int32)
    inside = (position[:, None] >= begins[None, :]) & (position[:, None] < prompt_end[None, :])
    starts = jnp.sum(jnp.where(inside, begins[None, :], 0), axis=1)
    return (position, starts)


def attend(query_block, key_rot, value_rows, pos_block, start_block, position):
    scores = jnp.einsum(
        "qkrd,skd->krqs", query_block, key_rot, preferred_element_type=jnp.float32
    ) * (1.0 / math.sqrt(HD))
    allowed = (position[None, :] <= pos_block[:, None]) & (
        position[None, :] >= start_block[:, None]
    )
    masked = jnp.where(allowed[None, None], scores, -jnp.inf)
    row_max = jnp.max(masked, axis=-1, keepdims=True)
    exp_scores = jnp.exp(masked - row_max)
    probs = (exp_scores / jnp.sum(exp_scores, axis=-1, keepdims=True)).astype(jnp.bfloat16)
    return jnp.einsum(
        "krqs,skd->qkrd", probs, value_rows, preferred_element_type=jnp.float32
    ).astype(jnp.bfloat16)


def with_zero_row(array):
    return jnp.concatenate([array, jnp.zeros((1,) + array.shape[1:], array.dtype)], axis=0)


def local(
    tokens,
    norm_gain,
    query_gain,
    key_gain,
    w_query,
    w_key,
    w_value,
    w_out,
    prompt_lengths,
    span_group,
):
    group_rows, width_local = tokens.shape
    groups = lax.axis_size("dp")
    arrival_rows = group_rows // groups
    capacity = 2 * arrival_rows
    device_index = lax.axis_index("dp")
    group_ids = jnp.arange(groups, dtype=jnp.int32)
    slot_ids = jnp.arange(capacity, dtype=jnp.int32)
    own_blocks = lax.dynamic_index_in_dim(span_group, device_index, 0, keepdims=False)
    counts = jnp.sum((span_group == device_index).astype(jnp.int32), axis=1)
    offsets = jnp.cumsum(counts) - counts
    row_dest = jnp.repeat(own_blocks, arrival_rows)
    onehot = (row_dest[:, None] == group_ids[None, :]).astype(jnp.int32)
    slot_rank = jnp.sum((jnp.cumsum(onehot, axis=0) - 1) * onehot, axis=1)
    send_slot = row_dest * capacity + slot_rank
    slot_source = (
        jnp.full((groups * capacity,), group_rows, jnp.int32)
        .at[send_slot]
        .set(jnp.arange(group_rows, dtype=jnp.int32))
    )
    outgoing = with_zero_row(tokens)[slot_source].reshape(groups, capacity, width_local)
    incoming = lax.all_to_all(outgoing, "dp", split_axis=0, concat_axis=0, tiled=True)
    is_valid = slot_ids[None, :] < arrival_rows * counts[:, None]
    target = arrival_rows * offsets[:, None] + slot_ids[None, :]
    flat_slot = group_ids[:, None] * capacity + slot_ids[None, :]
    back_index = jnp.where(is_valid, target, group_rows)
    source_of = (
        jnp.zeros((group_rows,), jnp.int32)
        .at[back_index.reshape(-1)]
        .set(flat_slot.reshape(-1), mode="drop")
    )
    arrived = incoming.reshape(groups * capacity, width_local)[source_of]
    full_rows = lax.all_gather(arrived, "fsdp", axis=1, tiled=True)
    query_full, key_full, value_full, out_full = (
        lax.all_gather(w_query, "dp", axis=0, tiled=True),
        lax.all_gather(w_key, "dp", axis=0, tiled=True),
        lax.all_gather(w_value, "dp", axis=0, tiled=True),
        lax.all_gather(w_out, "dp", axis=0, tiled=True),
    )
    lengths = lax.dynamic_index_in_dim(prompt_lengths, device_index, 0, keepdims=False)
    position, starts = prompt_layout(lengths, group_rows)
    within = position - starts
    floats = full_rows.astype(jnp.float32)
    normed = (
        floats
        * lax.rsqrt(jnp.mean(floats * floats, axis=-1, keepdims=True) + epsilon)
        * norm_gain.astype(jnp.float32)
    ).astype(jnp.bfloat16)
    query = jnp.dot(normed, query_full, preferred_element_type=jnp.float32).reshape(
        group_rows, -1, HD
    )
    key_rows = jnp.dot(normed, key_full, preferred_element_type=jnp.float32).reshape(
        group_rows, -1, HD
    )
    value_rows = (
        jnp.dot(normed, value_full, preferred_element_type=jnp.float32)
        .reshape(group_rows, -1, HD)
        .astype(jnp.bfloat16)
    )
    query_rot = rotate(head_norm(query, query_gain), within).astype(jnp.bfloat16)
    key_rot = rotate(head_norm(key_rows, key_gain), within).astype(jnp.bfloat16)
    kv_heads = key_rot.shape[1]
    group_ratio = QH // KVH
    cache_rows = jnp.concatenate([key_rot, value_rows], axis=-1)
    block_count = group_rows // 512
    block_len = group_rows // block_count
    query_heads = query_rot.reshape(block_count, block_len, kv_heads, group_ratio, HD)

    def one_block(pieces):
        query_block, pos_block, start_block = pieces
        return attend(query_block, key_rot, value_rows, pos_block, start_block, position)

    mixed = lax.map(
        one_block,
        (
            query_heads,
            position.reshape(block_count, block_len),
            starts.reshape(block_count, block_len),
        ),
    )
    mixed = mixed.reshape(group_rows, kv_heads * group_ratio * HD)
    heads_all = lax.all_gather(mixed, "fsdp", axis=1, tiled=True)
    update = jnp.dot(heads_all, out_full, preferred_element_type=jnp.float32).astype(jnp.bfloat16)
    arrays = (update, cache_rows)
    sent = tuple((with_zero_row(array)[back_index] for array in arrays))
    back = jax.tree.map(
        lambda part, own: part.astype(own.dtype),
        lax.all_to_all(for_sending(sent), "dp", split_axis=0, concat_axis=0, tiled=True),
        sent,
    )
    attention_out, cache_out = tuple(
        (piece.reshape((groups * capacity,) + piece.shape[2:])[send_slot] for piece in back)
    )
    return (attention_out, cache_out)


def solution(mesh):
    return jax.shard_map(
        local,
        mesh=mesh,
        in_specs=(
            P("dp", "fsdp"),
            P(),
            P(),
            P(),
            P("dp", "fsdp"),
            P("dp", "fsdp"),
            P("dp", "fsdp"),
            P("dp", "fsdp"),
            P(),
            P(),
        ),
        out_specs=(P("dp", "fsdp"), P("dp", "fsdp", None)),
        check_vma=False,
    )
```

profile of v0, /device:TPU:8, one launch (start us, length us, event | category | flops | bytes accessed | tf_op | source)
XLA Modules:
  0.0 579.5 jit_solution(6005886002139596010)
XLA Ops:
  8.9 18.0 %reduce-window.24 = s32[64,8,128]{2,1,0:T(8,128)S(1)} reduce-window(s32[64,8,128]{2,1,0:T(8,128)S(1)} %fusion.41, s32[]{:T(128)} %copy.68), window={size=1x1x128 pad=0_0x0_0x127_0}, to_apply=%region_0.1 | reduce-window | flops 8323072 | bytes 524292 | tf_op jit(solution)/shard_map/reduce-window
  27.8 4.3 scatter_custom_fusion
  32.2 1.1 concatenate.40
  33.3 9.0 %gather_fusion = bf16[2048,256]{1,0:T(8,128)(2,1)} fusion(bf16[1025,256]{1,0:T(8,128)(2,1)S(1)} %concatenate.40, s32[2048]{0:T(1024)S(1)} %fusion.43), kind=kCustom, calls=%fused_computation | custom fusion | bytes 2105344 | tf_op jit(solution)/shard_map/gather | solution.py:103
  42.3 18.9 %all-to-all-start = ((bf16[64,32,256]{2,1,0:T(8,128)(2,1)}), bf16[64,32,256]{2,1,0:T(8,128)(2,1)S(1)}, u32[]{:S(2)}, u32[]{:S(2)}) async-start(bf16[64,32,256]{2,1,0:T(8,128)(2,1)} %bitcast.9), calls=%async_computation | async-start | bytes 2097152 | tf_op jit(solution)/shard_map/all_to_all | solution.py:104
  62.0 8.0 %scatter_custom_fusion.1 = s32[1024]{0:T(1024)S(1)} fusion(s32[2048]{0:T(1024)S(1)} %bitcast.151, s32[2048]{0:T(1024)S(1)} %reshape.638, s32[]{:T(128)} %copy.68), kind=kCustom, calls=%fused_computation.100 | custom fusion | bytes 4100 | tf_op jit(solution)/shard_map/scatter | solution.py:112
  70.1 46.3 %all-to-all-done = bf16[64,32,256]{2,1,0:T(8,128)(2,1)S(1)} async-done(((bf16[64,32,256]{2,1,0:T(8,128)(2,1)}), bf16[64,32,256]{2,1,0:T(8,128)(2,1)S(1)}, u32[]{:S(2)}, u32[]{:S(2)}) %all-to-all-start) | async-done | bytes 1048608 | tf_op jit(solution)/shard_map/all_to_all | solution.py:104
  116.3 5.0 gather_fusion.1
  123.4 98.3 %all_gather.20 = bf16[2048,128]{1,0:T(8,128)(2,1)S(1)} all-gather(bf16[32,128]{1,0:T(8,128)(2,1)S(1)} %copy-done.4), channel_id=1, replica_groups=mesh['dp'=64,'fsdp'=8] {'dp'}, dimensions={0}, use_global_device_ids=true | all-gather | bytes 532480 | tf_op jit(solution)/shard_map/all_gather | solution.py:118
  221.7 98.6 %all_gather.21 = bf16[2048,128]{1,0:T(8,128)(2,1)S(1)} all-gather(bf16[32,128]{1,0:T(8,128)(2,1)S(1)} %copy-done.5), channel_id=1, replica_groups=mesh['dp'=64,'fsdp'=8] {'dp'}, dimensions={0}, use_global_device_ids=true | all-gather | bytes 532480 | tf_op jit(solution)/shard_map/all_gather | solution.py:119
  321.3 3.2 fusion.21
  325.8 1.5 multiply_reduce_fusion.1
  327.4 1.3 fusion.36
  328.8 1.5 fusion.27
  330.5 3.8 multiply_reduce_fusion
  336.5 9.5 %while.12 = (s32[]{:T(128)}, bf16[2,512,1,2,128]{4,3,1,0,2:T(2,128)(2,1)S(1)}, s32[2,512]{1,0:T(2,128)S(1)}, s32[2,512]{1,0:T(2,128)S(1)}, bf16[2,512,1,2,128]{4...) while((s32[]{:T(128)}, ...), condition=%wide.region_15.16_spmd.clone.clone, body=%wide.region_12.15_spmd.clone.clone.sunk | while | flops 551155712 | bytes 16285793 | solution.py:155
  337.1 1.0 fusion.70
  338.1 1.2 fusion.71
  339.3 1.6 fusion.72
  341.8 1.0 fusion.70
  342.9 1.2 fusion.71
  344.1 1.6 fusion.72
  347.3 9.0 %gather_fusion.4 = bf16[2048,256]{1,0:T(8,128)(2,1)} fusion(bf16[1025,256]{1,0:T(8,128)(2,1)S(1)} %copy.44, s32[2048]{0:T(1024)S(1)} %broadcast_clamp_fusion), kind=kCustom, calls=%fused_computation.4 | custom fusion | bytes 2105344 | tf_op jit(solution)/shard_map/gather | solution.py:167
  356.3 7.0 %all-to-all-start.2 = ((bf16[64,32,1,256]{3,1,2,0:T(8,128)(2,1)}), bf16[64,32,1,256]{3,1,2,0:T(8,128)(2,1)S(1)}, u32[]{:S(2)}, u32[]{:S(2)}) async-start(bf16[64,32,1,256]{3,1,2,0:T(8,128)(2,1)} %bitcast.20), calls=%async_computation.2 | async-start | bytes 2097152 | tf_op jit(solution)/shard_map/all_to_all | solution.py:170
  363.3 77.8 %all-gather.10.cloned.1.call-done = bf16[2048,256]{1,0:T(8,128)(2,1)} async-done(((bf16[32,256]{1,0:T(8,128)(2,1)}), bf16[2048,256]{1,0:T(8,128)(2,1)}) %all-gather.10.cloned.1.call-update) | async-done | bytes 1048592 | tf_op jit(solution)/shard_map/all_gather | solution.py:120
  441.1 42.8 %all-gather.8.cloned.1.call-done = bf16[1024,2048]{1,0:T(8,128)(2,1)} async-done(((bf16[1024,256]{1,0:T(8,128)(2,1)}), bf16[1024,2048]{1,0:T(8,128)(2,1)}) %all-gather.8.cloned.1.call-update) | async-done | bytes 4194320 | tf_op jit(solution)/shard_map/all_gather | solution.py:164
  483.9 3.7 convolution_convert_fusion
  487.7 9.0 %gather_fusion.2 = bf16[2048,256]{1,0:T(8,128)(2,1)} fusion(bf16[1025,256]{1,0:T(8,128)(2,1)S(1)} %concatenate.45, s32[2048]{0:T(1024)S(1)} %broadcast_clamp_fusion), kind=kCustom, calls=%fused_computation.2 | custom fusion | bytes 2105344 | tf_op jit(solution)/shard_map/gather | solution.py:167
  496.7 15.7 %all-to-all-start.1 = ((bf16[64,32,256]{2,1,0:T(8,128)(2,1)}), bf16[64,32,256]{2,1,0:T(8,128)(2,1)S(1)}, u32[]{:S(2)}, u32[]{:S(2)}) async-start(bf16[64,32,256]{2,1,0:T(8,128)(2,1)} %bitcast.16), calls=%async_computation.1 | async-start | bytes 2097152 | tf_op jit(solution)/shard_map/all_to_all | solution.py:170
  512.5 5.0 gather_fusion.5
  517.4 50.6 %all-to-all-done.1 = bf16[64,32,256]{2,1,0:T(8,128)(2,1)S(1)} async-done(((bf16[64,32,256]{2,1,0:T(8,128)(2,1)}), bf16[64,32,256]{2,1,0:T(8,128)(2,1)S(1)}, u32[]{:S(2)}, u32[]{:S(2)}) %all-to-all-start.1) | async-done | bytes 1048608 | tf_op jit(solution)/shard_map/all_to_all | solution.py:170
  568.0 5.0 gather_fusion.3
  (103 shorter events, 13.2 us)
Async XLA Ops:
  7.2 115.7 %copy-start = (s32[64,8]{0,1:T(8,128)S(1)}, s32[64,8]{0,1:T(8,128)}, u32[]{:S(2)}) copy-start(s32[64,8]{0,1:T(8,128)} %param.20) | copy-start | bytes 6148
  33.2 28.0 %copy-start.3 = (s32[64,64]{1,0:T(8,128)S(1)}, s32[64,64]{1,0:T(8,128)}, u32[]{:S(2)}) copy-start(s32[64,64]{1,0:T(8,128)} %param.21) | copy-start | bytes 49156
  42.3 81.1 %copy-start.6 = (bf16[2048]{0:T(1024)(128)(2,1)S(1)}, bf16[2048]{0:T(1024)(128)(2,1)}, u32[]{:S(2)}) copy-start(bf16[2048]{0:T(1024)(128)(2,1)} %param.13) | copy-start | bytes 12292
  42.3 81.1 %copy-start.4 = (bf16[32,128]{1,0:T(8,128)(2,1)S(1)}, bf16[32,128]{1,0:T(8,128)(2,1)}, u32[]{:S(2)}) copy-start(bf16[32,128]{1,0:T(8,128)(2,1)} %param.17) | copy-start | bytes 24580
  42.3 179.4 %copy-start.7 = (bf16[128]{0:T(256)(128)(2,1)S(1)}, bf16[128]{0:T(256)(128)(2,1)}, u32[]{:S(2)}) copy-start(bf16[128]{0:T(256)(128)(2,1)} %param.15) | copy-start | bytes 772
  42.3 179.4 %copy-start.5 = (bf16[32,128]{1,0:T(8,128)(2,1)S(1)}, bf16[32,128]{1,0:T(8,128)(2,1)}, u32[]{:S(2)}) copy-start(bf16[32,128]{1,0:T(8,128)(2,1)} %param.18) | copy-start | bytes 24580
  42.3 278.0 %copy-start.8 = (bf16[128]{0:T(256)(128)(2,1)S(1)}, bf16[128]{0:T(256)(128)(2,1)}, u32[]{:S(2)}) copy-start(bf16[128]{0:T(256)(128)(2,1)} %param.14) | copy-start | bytes 772
  42.3 74.0 %all-to-all-start = ((bf16[64,32,256]{2,1,0:T(8,128)(2,1)}), bf16[64,32,256]{2,1,0:T(8,128)(2,1)S(1)}, u32[]{:S(2)}, u32[]{:S(2)}) async-start(bf16[64,32,256]{2,1,0:T(8,128)(2,1)} %bitcast.9), calls=%async_computation | async-start | bytes 2097152 | tf_op jit(solution)/shard_map/all_to_all | solution.py:104
  61.2 260.1 %all-gather.12.cloned.1.call-start = ((), (), s32[]{:S(2)}) async-start(), calls=%async_computation.6 | async-start | bytes 4718592 | tf_op jit(solution)/shard_map/all_gather | solution.py:115
  121.3 209.2 %all-gather.6.cloned.1.call-start = ((), (), s32[]{:S(2)}) async-start(), calls=%async_computation.3 | async-start | bytes 1064960 | tf_op jit(solution)/shard_map/all_gather | solution.py:117
  122.1 319.0 %all-gather.10.cloned.1.call-start = ((), (), s32[]{:S(2)}) async-start(), calls=%async_computation.5 | async-start | bytes 1064960 | tf_op jit(solution)/shard_map/all_gather | solution.py:120
  122.8 361.1 %all-gather.8.cloned.1.call-start = ((), (), s32[]{:S(2)}) async-start(), calls=%async_computation.4 | async-start | bytes 4718592 | tf_op jit(solution)/shard_map/all_gather | solution.py:164
  321.3 3.5 copy-start.2
  325.8 4.6 copy-start.1
  356.3 140.4 %all-to-all-start.2 = ((bf16[64,32,1,256]{3,1,2,0:T(8,128)(2,1)}), bf16[64,32,1,256]{3,1,2,0:T(8,128)(2,1)S(1)}, u32[]{:S(2)}, u32[]{:S(2)}) async-start(bf16[64,32,1,256]{3,1,2,0:T(8,128)(2,1)} %bitcast.20), calls=%async_computation.2 | async-start | bytes 2097152 | tf_op jit(solution)/shard_map/all_to_all | solution.py:170
  496.7 71.3 %all-to-all-start.1 = ((bf16[64,32,256]{2,1,0:T(8,128)(2,1)}), bf16[64,32,256]{2,1,0:T(8,128)(2,1)S(1)}, u32[]{:S(2)}, u32[]{:S(2)}) async-start(bf16[64,32,256]{2,1,0:T(8,128)(2,1)} %bitcast.16), calls=%async_computation.1 | async-start | bytes 2097152 | tf_op jit(solution)/shard_map/all_to_all | solution.py:170
Sparse Core Ops, SparseCore 0:
  121.5 34.7 all-gather.11
  159.2 139.9 all-gather.5
  302.1 138.9 all-gather.9
  443.6 40.2 all-gather.7
where the time goes:
time: 580 us
  waiting for transfers between devices  219 us (38%)
  blocking collectives  197 us (34%)
  local copies, waits for them, and re-layouts  60.6 us (10%)
  starting transfers between devices  41.7 us (7%)
  other arithmetic  31.2 us (5%)
  matrix products  15.8 us (3%)
  between operations  14.3 us (2%)
    all_gather x1, blocking collectives, local(): lax.all_gather(w_value, 'dp', axis=0, tiled=True)  98.6 us
    all_gather x1, blocking collectives, local(): lax.all_gather(w_key, 'dp', axis=0, tiled=True)  98.3 us
    all_gather x1, waiting for transfers between devices, local(): lax.all_gather(w_out, 'dp', axis=0, tiled=True)  77.8 us
    all_to_all x2, waiting for transfers between devices, local(): lax.all_to_all(for_sending(sent), 'dp', split_axis=0, concat_axis=0, tile...  50.6 us
    all_to_all x1, waiting for transfers between devices, local(): lax.all_to_all(outgoing, 'dp', split_axis=0, concat_axis=0, tiled=True)  46.3 us
    all_gather x1, waiting for transfers between devices, local(): heads_all = lax.all_gather(mixed, 'fsdp', axis=1, tiled=True)  42.8 us
    all_to_all x2, starting transfers between devices, local(): lax.all_to_all(for_sending(sent), 'dp', split_axis=0, concat_axis=0, tile...  22.7 us
    another operation x7, other arithmetic  19.9 us
  transfers between devices with their start and end apart: 7, of which 4 were waited for; matrix products, arithmetic and copies ran while one was open for 11% of the time, Pallas kernels for 0%

commit v1 on v0

--- a/solution.py
+++ b/solution.py
@@ -115,7 +115,9 @@
     full_rows = lax.all_gather(arrived, "fsdp", axis=1, tiled=True)
     query_full, key_full, value_full, out_full = (
         lax.all_gather(w_query, "dp", axis=0, tiled=True),
-        lax.all_gather(w_key, "dp", axis=0, tiled=True),
+        jnp.concatenate(
+            lax.all_to_all(jnp.stack([w_key] * lax.axis_size("dp")), "dp", 0, 0), axis=0
+        ),
         lax.all_gather(w_value, "dp", axis=0, tiled=True),
         lax.all_gather(w_out, "dp", axis=0, tiled=True),
     )

time: 580 us -> 581 us (level)
  blocking collectives: 197 us -> 116 us
  waiting for transfers between devices: 219 us -> 285 us
  starting transfers between devices: 41.7 us -> 52.2 us
    all_gather x1 -> x0, blocking collectives: 98.3 us -> none  [local(): lax.all_gather(w_key, 'dp', axis=0, tiled=True)]
    all_gather x1, waiting for transfers between devices: 0.02 us -> 38.9 us  [local(): lax.all_gather(w_query, 'dp', axis=0, tiled=True)]
    all_gather x1, waiting for transfers between devices: 77.8 us -> 105 us  [local(): lax.all_gather(w_out, 'dp', axis=0, tiled=True)]
    all_gather x1, blocking collectives: 98.6 us -> 116 us  [local(): lax.all_gather(w_value, 'dp', axis=0, tiled=True)]
    all_to_all x0 -> x1, starting transfers between devices: none -> 5.95 us  [local(): lax.all_to_all(jnp.stack([w_key] * lax.axis_size('dp')), 'dp', 0, 0)]
  transfers between devices with their start and end apart: 7 -> 8, of which waited for: 4 -> 5; matrix products, arithmetic and copies ran while one was open for 11% -> 12% of each run, Pallas kernels for 0% -> 0%
where the time goes in v1:
time: 581 us; the launch traced here: 580 us
  waiting for transfers between devices  285 us (49%)
  blocking collectives  116 us (20%)
  local copies, waits for them, and re-layouts  61.5 us (11%)
  starting transfers between devices  52.2 us (9%)
  other arithmetic  33.2 us (6%)
  matrix products  18.2 us (3%)
  between operations  14.3 us (2%)
    all_gather x1, blocking collectives, local(): lax.all_gather(w_value, 'dp', axis=0, tiled=True)  116 us
    all_gather x1, waiting for transfers between devices, local(): lax.all_gather(w_out, 'dp', axis=0, tiled=True)  105 us
    all_to_all x2, waiting for transfers between devices, local(): lax.all_to_all(for_sending(sent), 'dp', split_axis=0, concat_axis=0, tile...  50.6 us
    all_to_all x1, waiting for transfers between devices, local(): lax.all_to_all(outgoing, 'dp', split_axis=0, concat_axis=0, tiled=True)  46.3 us
    all_gather x1, waiting for transfers between devices, local(): heads_all = lax.all_gather(mixed, 'fsdp', axis=1, tiled=True)  42.8 us
    all_gather x1, waiting for transfers between devices, local(): lax.all_gather(w_query, 'dp', axis=0, tiled=True)  38.9 us
    all_to_all x2, starting transfers between devices, local(): lax.all_to_all(for_sending(sent), 'dp', split_axis=0, concat_axis=0, tile...  27.2 us
    another operation x7, other arithmetic  20 us
  transfers between devices with their start and end apart: 8, of which 5 were waited for; matrix products, arithmetic and copies ran while one was open for 12% of the time, Pallas kernels for 0%

profile of v1, /device:TPU:8, one launch (start us, length us, event | category | flops | bytes accessed | tf_op | source)
XLA Modules:
  0.0 580.1 jit_solution(12361006603699269954)
XLA Ops:
  8.9 18.0 %reduce-window.24 = s32[64,8,128]{2,1,0:T(8,128)S(1)} reduce-window(s32[64,8,128]{2,1,0:T(8,128)S(1)} %fusion.41, s32[]{:T(128)} %copy.68), window={size=1x1x128 pad=0_0x0_0x127_0}, to_apply=%region_0.1 | reduce-window | flops 8323072 | bytes 524292 | tf_op jit(solution)/shard_map/reduce-window
  27.8 4.3 scatter_custom_fusion
  32.2 1.1 concatenate.40
  33.3 9.0 %gather_fusion = bf16[2048,256]{1,0:T(8,128)(2,1)} fusion(bf16[1025,256]{1,0:T(8,128)(2,1)S(1)} %concatenate.40, s32[2048]{0:T(1024)S(1)} %fusion.43), kind=kCustom, calls=%fused_computation | custom fusion | bytes 2105344 | tf_op jit(solution)/shard_map/gather | solution.py:103
  42.3 18.9 %all-to-all-start = ((bf16[64,32,256]{2,1,0:T(8,128)(2,1)}), bf16[64,32,256]{2,1,0:T(8,128)(2,1)S(1)}, u32[]{:S(2)}, u32[]{:S(2)}) async-start(bf16[64,32,256]{2,1,0:T(8,128)(2,1)} %bitcast.9), calls=%async_computation | async-start | bytes 2097152 | tf_op jit(solution)/shard_map/all_to_all | solution.py:104
  62.0 8.0 %scatter_custom_fusion.1 = s32[1024]{0:T(1024)S(1)} fusion(s32[2048]{0:T(1024)S(1)} %bitcast.153, s32[2048]{0:T(1024)S(1)} %reshape.644, s32[]{:T(128)} %copy.68), kind=kCustom, calls=%fused_computation.100 | custom fusion | bytes 4100 | tf_op jit(solution)/shard_map/scatter | solution.py:112
  70.1 46.3 %all-to-all-done = bf16[64,32,256]{2,1,0:T(8,128)(2,1)S(1)} async-done(((bf16[64,32,256]{2,1,0:T(8,128)(2,1)}), bf16[64,32,256]{2,1,0:T(8,128)(2,1)S(1)}, u32[]{:S(2)}, u32[]{:S(2)}) %all-to-all-start) | async-done | bytes 1048608 | tf_op jit(solution)/shard_map/all_to_all | solution.py:104
  116.3 5.0 gather_fusion.1
  123.0 6.0 %all-to-all-start.1 = ((bf16[64,32,128]{2,1,0:T(8,128)(2,1)}), bf16[64,32,128]{2,1,0:T(8,128)(2,1)S(1)}, u32[]{:S(2)}, u32[]{:S(2)}) async-start(bf16[64,32,128]{2,1,0:T(8,128)(2,1)} %stack.2), calls=%async_computation.1 | async-start | bytes 1048576 | tf_op jit(solution)/shard_map/all_to_all | solution.py:119
  130.3 115.5 %all_gather.17 = bf16[2048,128]{1,0:T(8,128)(2,1)S(1)} all-gather(bf16[32,128]{1,0:T(8,128)(2,1)S(1)} %copy-done.5), channel_id=1, replica_groups=mesh['dp'=64,'fsdp'=8] {'dp'}, dimensions={0}, use_global_device_ids=true | all-gather | bytes 532480 | tf_op jit(solution)/shard_map/all_gather | solution.py:121
  246.8 3.2 fusion.21
  250.3 2.9 fusion.23
  253.2 3.9 multiply_reduce_fusion.1
  257.2 1.3 fusion.36
  258.6 1.5 fusion.27
  260.3 38.9 %all-gather.6.cloned.1.call-done = bf16[2048,256]{1,0:T(8,128)(2,1)} async-done(((bf16[32,256]{1,0:T(8,128)(2,1)}), bf16[2048,256]{1,0:T(8,128)(2,1)}) %all-gather.6.cloned.1.call-update) | async-done | bytes 1048592 | tf_op jit(solution)/shard_map/all_gather | solution.py:117
  299.2 3.8 multiply_reduce_fusion
  305.1 9.5 %while.12 = (s32[]{:T(128)}, bf16[2,512,1,2,128]{4,3,1,0,2:T(2,128)(2,1)S(1)}, s32[2,512]{1,0:T(2,128)S(1)}, s32[2,512]{1,0:T(2,128)S(1)}, bf16[2,512,1,2,128]{4...) while((s32[]{:T(128)}, ...), condition=%wide.region_15.16_spmd.clone.clone, body=%wide.region_12.15_spmd.clone.clone.sunk | while | flops 551155712 | bytes 16285793 | solution.py:157
  306.8 1.2 fusion.71
  307.9 1.6 fusion.72
  311.5 1.2 fusion.71
  312.7 1.6 fusion.72
  315.9 9.0 %gather_fusion.4 = bf16[2048,256]{1,0:T(8,128)(2,1)} fusion(bf16[1025,256]{1,0:T(8,128)(2,1)S(1)} %copy.44, s32[2048]{0:T(1024)S(1)} %broadcast_clamp_fusion), kind=kCustom, calls=%fused_computation.4 | custom fusion | bytes 2105344 | tf_op jit(solution)/shard_map/gather | solution.py:169
  324.9 11.5 %all-to-all-start.3 = ((bf16[64,32,1,256]{3,1,2,0:T(8,128)(2,1)}), bf16[64,32,1,256]{3,1,2,0:T(8,128)(2,1)S(1)}, u32[]{:S(2)}, u32[]{:S(2)}) async-start(bf16[64,32,1,256]{3,1,2,0:T(8,128)(2,1)} %bitcast.21), calls=%async_computation.3 | async-start | bytes 2097152 | tf_op jit(solution)/shard_map/all_to_all | solution.py:172
  336.4 105.3 %all-gather.10.cloned.1.call-done = bf16[2048,256]{1,0:T(8,128)(2,1)} async-done(((bf16[32,256]{1,0:T(8,128)(2,1)}), bf16[2048,256]{1,0:T(8,128)(2,1)}) %all-gather.10.cloned.1.call-update) | async-done | bytes 1048592 | tf_op jit(solution)/shard_map/all_gather | solution.py:122
  441.7 42.8 %all-gather.8.cloned.1.call-done = bf16[1024,2048]{1,0:T(8,128)(2,1)} async-done(((bf16[1024,256]{1,0:T(8,128)(2,1)}), bf16[1024,2048]{1,0:T(8,128)(2,1)}) %all-gather.8.cloned.1.call-update) | async-done | bytes 4194320 | tf_op jit(solution)/shard_map/all_gather | solution.py:166
  484.5 3.7 convolution_convert_fusion
  488.3 9.0 %gather_fusion.2 = bf16[2048,256]{1,0:T(8,128)(2,1)} fusion(bf16[1025,256]{1,0:T(8,128)(2,1)S(1)} %concatenate.45, s32[2048]{0:T(1024)S(1)} %broadcast_clamp_fusion), kind=kCustom, calls=%fused_computation.2 | custom fusion | bytes 2105344 | tf_op jit(solution)/shard_map/gather | solution.py:169
  497.3 15.7 %all-to-all-start.2 = ((bf16[64,32,256]{2,1,0:T(8,128)(2,1)}), bf16[64,32,256]{2,1,0:T(8,128)(2,1)S(1)}, u32[]{:S(2)}, u32[]{:S(2)}) async-start(bf16[64,32,256]{2,1,0:T(8,128)(2,1)} %bitcast.17), calls=%async_computation.2 | async-start | bytes 2097152 | tf_op jit(solution)/shard_map/all_to_all | solution.py:172
  513.1 5.0 gather_fusion.5
  518.0 50.6 %all-to-all-done.2 = bf16[64,32,256]{2,1,0:T(8,128)(2,1)S(1)} async-done(((bf16[64,32,256]{2,1,0:T(8,128)(2,1)}), bf16[64,32,256]{2,1,0:T(8,128)(2,1)S(1)}, u32[]{:S(2)}, u32[]{:S(2)}) %all-to-all-start.2) | async-done | bytes 1048608 | tf_op jit(solution)/shard_map/all_to_all | solution.py:172
  568.6 5.0 gather_fusion.3
  (105 shorter events, 15.1 us)
Async XLA Ops:
  7.2 122.6 %copy-start = (s32[64,8]{0,1:T(8,128)S(1)}, s32[64,8]{0,1:T(8,128)}, u32[]{:S(2)}) copy-start(s32[64,8]{0,1:T(8,128)} %param.20) | copy-start | bytes 6148
  33.2 28.0 %copy-start.3 = (s32[64,64]{1,0:T(8,128)S(1)}, s32[64,64]{1,0:T(8,128)}, u32[]{:S(2)}) copy-start(s32[64,64]{1,0:T(8,128)} %param.21) | copy-start | bytes 49156
  42.3 79.8 %copy-start.4 = (bf16[32,128]{1,0:T(8,128)(2,1)S(1)}, bf16[32,128]{1,0:T(8,128)(2,1)}, u32[]{:S(2)}) copy-start(bf16[32,128]{1,0:T(8,128)(2,1)} %param.17) | copy-start | bytes 24580
  42.3 87.5 %copy-start.6 = (bf16[2048]{0:T(1024)(128)(2,1)S(1)}, bf16[2048]{0:T(1024)(128)(2,1)}, u32[]{:S(2)}) copy-start(bf16[2048]{0:T(1024)(128)(2,1)} %param.13) | copy-start | bytes 12292
  42.3 87.5 %copy-start.7 = (bf16[128]{0:T(256)(128)(2,1)S(1)}, bf16[128]{0:T(256)(128)(2,1)}, u32[]{:S(2)}) copy-start(bf16[128]{0:T(256)(128)(2,1)} %param.15) | copy-start | bytes 772
  42.3 87.9 %copy-start.8 = (bf16[128]{0:T(256)(128)(2,1)S(1)}, bf16[128]{0:T(256)(128)(2,1)}, u32[]{:S(2)}) copy-start(bf16[128]{0:T(256)(128)(2,1)} %param.14) | copy-start | bytes 772
  42.3 88.0 %copy-start.5 = (bf16[32,128]{1,0:T(8,128)(2,1)S(1)}, bf16[32,128]{1,0:T(8,128)(2,1)}, u32[]{:S(2)}) copy-start(bf16[32,128]{1,0:T(8,128)(2,1)} %param.18) | copy-start | bytes 24580
  42.3 74.1 %all-to-all-start = ((bf16[64,32,256]{2,1,0:T(8,128)(2,1)}), bf16[64,32,256]{2,1,0:T(8,128)(2,1)S(1)}, u32[]{:S(2)}, u32[]{:S(2)}) async-start(bf16[64,32,256]{2,1,0:T(8,128)(2,1)} %bitcast.9), calls=%async_computation | async-start | bytes 2097152 | tf_op jit(solution)/shard_map/all_to_all | solution.py:104
  61.2 185.7 %all-gather.12.cloned.1.call-start = ((), (), s32[]{:S(2)}) async-start(), calls=%async_computation.7 | async-start | bytes 4718592 | tf_op jit(solution)/shard_map/all_gather | solution.py:115
  121.3 177.8 %all-gather.6.cloned.1.call-start = ((), (), s32[]{:S(2)}) async-start(), calls=%async_computation.4 | async-start | bytes 1064960 | tf_op jit(solution)/shard_map/all_gather | solution.py:117
  123.0 130.3 %all-to-all-start.1 = ((bf16[64,32,128]{2,1,0:T(8,128)(2,1)}), bf16[64,32,128]{2,1,0:T(8,128)(2,1)S(1)}, u32[]{:S(2)}, u32[]{:S(2)}) async-start(bf16[64,32,128]{2,1,0:T(8,128)(2,1)} %stack.2), calls=%async_computation.1 | async-start | bytes 1048576 | tf_op jit(solution)/shard_map/all_to_all | solution.py:119
  128.9 312.8 %all-gather.10.cloned.1.call-start = ((), (), s32[]{:S(2)}) async-start(), calls=%async_computation.6 | async-start | bytes 1064960 | tf_op jit(solution)/shard_map/all_gather | solution.py:122
  129.7 354.9 %all-gather.8.cloned.1.call-start = ((), (), s32[]{:S(2)}) async-start(), calls=%async_computation.5 | async-start | bytes 4718592 | tf_op jit(solution)/shard_map/all_gather | solution.py:166
  246.8 3.5 copy-start.2
  253.2 5.4 copy-start.1
  324.9 172.4 %all-to-all-start.3 = ((bf16[64,32,1,256]{3,1,2,0:T(8,128)(2,1)}), bf16[64,32,1,256]{3,1,2,0:T(8,128)(2,1)S(1)}, u32[]{:S(2)}, u32[]{:S(2)}) async-start(bf16[64,32,1,256]{3,1,2,0:T(8,128)(2,1)} %bitcast.21), calls=%async_computation.3 | async-start | bytes 2097152 | tf_op jit(solution)/shard_map/all_to_all | solution.py:172
  497.3 71.3 %all-to-all-start.2 = ((bf16[64,32,256]{2,1,0:T(8,128)(2,1)}), bf16[64,32,256]{2,1,0:T(8,128)(2,1)S(1)}, u32[]{:S(2)}, u32[]{:S(2)}) async-start(bf16[64,32,256]{2,1,0:T(8,128)(2,1)} %bitcast.17), calls=%async_computation.2 | async-start | bytes 2097152 | tf_op jit(solution)/shard_map/all_to_all | solution.py:172
Sparse Core Ops, SparseCore 0:
  121.5 34.9 all-gather.11
  159.4 139.7 all-gather.5
  302.1 139.5 all-gather.9
  444.2 40.2 all-gather.7
